TPU v7x, 512 devices: a whole 4x8x8 slice. The times are simulated.
512 devices in a mesh: space: 64 (over z_lo, y, core), chan: 8 (over x, z_hi).
Axes of the slice: x: 4, y: 8, z: 8 (z_hi: 2, z_lo: 4; z = z_hi * 4 + z_lo), core: 2. Of those that a mesh axis runs over, the one named last changes fastest.
Arguments:
- features: bfloat16 [1, 128, 128, 2048], P(None, 'chan', 'space'), may hold values from -6 to 6
- top_map: int32 [64, 2048], P('space'), may hold values from 0 to 2048, as said below
- bottom_map: int32 [64, 2048], P('space'), may hold values from 0 to 2048, as said below
- first_weight: bfloat16 [128, 3, 3, 128], P('chan'), may hold values from -0.1875 to 0.1875
- first_bias: float32 [128], P('chan'), may hold values from -3 to 3
- second_weight: bfloat16 [256, 3, 3, 128], P('chan'), may hold values from -0.1875 to 0.1875
- second_bias: float32 [256], P('chan'), may hold values from -3 to 3
Outputs:
- hidden: bfloat16 [1, 128, 128, 2048], P(None, 'chan', 'space')
- coarse: bfloat16 [1, 256, 64, 1024], P(None, 'chan', 'space')
Inputs may be any that keep to these rules, and one draw needn't show every extreme that they name: `top_map`: each entry of row s, column k is k - 1, k or k + 1 taken modulo 2048, or 2048 for a missing neighbour at a face corner; exactly 4 entries of each row equal 2048. `bottom_map`: each entry of row s, column k is k - 1, k or k + 1 taken modulo 2048, or 2048 for a missing neighbour at a face corner; exactly 4 entries of each row equal 2048.
All inputs are finite; a program needn't handle non-finite values.
Results may differ from a plain program's by a relative error of at most 0.012.
Values may be sent and summed in bfloat16 or wider, within the bound.
No kernel may reach another device: no remote copies, remote signals or barrier semaphores. Data moves between devices by JAX's collectives and lax.ppermute only.
A program may use at most 64 MiB of HBM per device.

v0:
```python
import jax
import jax.numpy as jnp
from jax import lax
from jax.sharding import PartitionSpec as P


def with_halo(cells, sides, width):
    for axis, dim in sides:
        count = lax.axis_size(axis)
        ends = count - 1
        head = lax.slice_in_dim(cells, 0, width, axis=dim)
        tail = lax.slice_in_dim(cells, cells.shape[dim] - width, cells.shape[dim], axis=dim)
        cells = jnp.concatenate(
            [
                lax.ppermute(tail, axis, [(i, (i + 1) % count) for i in range(ends)]),
                cells,
                lax.ppermute(head, axis, [((i + 1) % count, i) for i in range(ends)]),
            ],
            axis=dim,
        )
    return cells


def shifted_2(array, axis, by):
    devices = lax.axis_size(axis)
    pairs = [(i, i + by) for i in range(devices) if 0 <= i + by < devices]
    return lax.ppermute(array, axis, pairs)


def remap_row(source_row, table):
    zero_col = jnp.zeros(source_row.shape[:-1] + (1,), source_row.dtype)
    return jnp.take(jnp.concatenate([source_row, zero_col], axis=-1), table, axis=-1)


def per_device(features, top_map, bottom_map, first_weight, first_bias, second_weight, second_bias):
    row_count = features.shape[2]
    cycle_width = features.shape[3]
    upper_map = top_map[0]
    lower_map = bottom_map[0]
    gathered = lax.all_gather(features, "chan", axis=1, tiled=True)
    framed = with_halo(gathered, (("space", 2),), 1)
    above_row = remap_row(framed[:, :, 0, :], upper_map)
    below_row = remap_row(framed[:, :, row_count + 1, :], lower_map)
    padded = jnp.concatenate([above_row[:, :, None], gathered, below_row[:, :, None]], 2)
    totals = jnp.zeros(
        (features.shape[0], first_weight.shape[0], row_count, cycle_width), jnp.float32
    )
    for row_step in range(3):
        for col_step in range(3):
            shifted = jnp.roll(
                padded[:, :, row_step : row_step + row_count, :], 1 - col_step, axis=3
            )
            totals = totals + jnp.einsum(
                "oc,bcrw->borw",
                first_weight[:, row_step, col_step, :],
                shifted,
                preferred_element_type=jnp.float32,
            )
    hidden = jax.nn.gelu(totals + first_bias[None, :, None, None]).astype(jnp.bfloat16)
    half_rows = row_count // 2
    gathered_hidden = lax.all_gather(hidden, "chan", axis=1, tiled=True)
    rim_row = shifted_2(gathered_hidden[:, :, row_count - 1, :], "space", 1)
    stacked = jnp.concatenate([remap_row(rim_row, upper_map)[:, :, None], gathered_hidden], 2)
    sums = jnp.zeros(
        (hidden.shape[0], second_weight.shape[0], half_rows, cycle_width // 2), jnp.float32
    )
    for row_step in range(3):
        for col_step in range(3):
            picked = jnp.roll(
                stacked[:, :, row_step : row_step + row_count : 2, :], 1 - col_step, axis=3
            )[..., ::2]
            sums = sums + jnp.einsum(
                "oc,bcrw->borw",
                second_weight[:, row_step, col_step, :],
                picked,
                preferred_element_type=jnp.float32,
            )
    coarse = jax.nn.gelu(sums + second_bias[None, :, None, None]).astype(jnp.bfloat16)
    return (hidden, coarse)


def solution(mesh):
    placed = (
        P(None, "chan", "space", None),
        P("space", None),
        P("space", None),
        P("chan", None, None, None),
        P("chan"),
        P("chan", None, None, None),
        P("chan"),
    )
    return jax.shard_map(
        per_device,
        mesh=mesh,
        in_specs=placed,
        out_specs=(P(None, "chan", "space", None), P(None, "chan", "space", None)),
        check_vma=False,
    )
```

profile of v0, /device:TPU:25, one launch (start us, length us, event | category | flops | bytes accessed | tf_op | source)
XLA Modules:
  0.0 264.1 jit_solution(7621877287431449558)
XLA Ops:
  7.2 0.0 all-gather.3.cloned.1.call-start
  7.2 1.6 copy.9
  8.8 0.0 all-gather.5.cloned.1.call-start
  8.9 0.7 compare_and_fusion.1
  9.6 0.7 fusion.97
  10.3 72.2 %all-gather.3.cloned.1.call-done = bf16[1,128,2,2048]{3,1,2,0:T(8,128)(2,1)} async-done(((bf16[1,16,2,2048]{3,1,2,0:T(8,128)(2,1)}), bf16[1,128,2,2048]{3,1,2,0:T(8,128)(2,1)}) %all-gather.3.cloned.1.call-update) | async-done | bytes 1048592 | tf_op jit(solution)/shard_map/all_gather | solution.py:40
  82.5 2.2 fusion.128
  84.7 6.3 %collective-permute-start = (bf16[1,128,1,2048]{3,1,2,0:T(8,128)(2,1)S(1)}, bf16[1,128,1,2048]{3,1,2,0:T(8,128)(2,1)S(1)}, u32[]{:S(2)}, u32[]{:S(2)}) collective-permute-start(bf16[1,128,1,2048]{3,1,2,0:T(8,128)(2,1)S(1)} %get-tuple-element.25), channel_id=1, source_target_pairs={{0,8},{8,16},{16,24},{24,32},{32,40},{40,48},{48,56},{56,64},{64,7... | collective-permute-start | bytes 1572872 | tf_op jit(solution)/shard_map/ppermute | solution.py:15
  91.0 1.9 collective-permute-start.1
  92.9 0.1 fusion.129
  93.0 4.0 %collective-permute-done = bf16[1,128,1,2048]{3,1,2,0:T(8,128)(2,1)S(1)} collective-permute-done((bf16[1,128,1,2048]{3,1,2,0:T(8,128)(2,1)S(1)}, bf16[1,128,1,2048]{3,1,2,0:T(8,128)(2,1)S(1)}, u32[]{:S(2)}, u32[]{:S(2)}) %collective-permute-start) | collective-permute-done | bytes 524320 | tf_op jit(solution)/shard_map/ppermute | solution.py:15
  97.1 0.3 copy.10
  97.4 6.2 %gather_fusion = bf16[2048,128]{1,0:T(8,128)(2,1)S(1)} fusion(bf16[128,2049]{0,1:T(8,128)(2,1)S(1)} %copy.10, s32[2048]{0:T(1024)S(1)} %fusion.97), kind=kCustom, calls=%fused_computation.clone | custom fusion | bytes 1056768 | tf_op jit(solution)/shard_map/jit(_take)/gather | solution.py:32
  103.6 0.2 copy.11
  103.9 0.3 copy.12
  104.2 6.2 %gather_fusion.1 = bf16[2048,128]{1,0:T(8,128)(2,1)S(1)} fusion(bf16[128,2049]{0,1:T(8,128)(2,1)S(1)} %copy.12, s32[2048]{0:T(1024)S(1)} %fusion.98), kind=kCustom, calls=%fused_computation.1.clone | custom fusion | bytes 1056768 | tf_op jit(solution)/shard_map/jit(_take)/gather | solution.py:32
  110.4 0.2 copy.13
  110.6 0.1 fusion.43
  110.7 1.4 fusion.6
  112.2 0.5 fusion.30
  112.7 0.3 convolution_add_fusion.7
  112.9 0.3 convolution_add_fusion.6
  113.2 0.5 convolution_add_fusion.5
  113.7 0.3 convolution_add_fusion.4
  113.9 0.3 convolution_add_fusion.3
  114.2 0.5 convolution_add_fusion.2
  114.7 0.3 convolution_add_fusion.1
  115.0 0.4 copy-done.6
  115.4 0.9 fusion.54
  116.3 1.7 copy.15
  118.0 61.1 %all-gather.5.cloned.1.call-done = bf16[1,128,2,2048]{3,1,2,0:T(8,128)(2,1)} async-done(((bf16[1,16,2,2048]{3,1,2,0:T(8,128)(2,1)}), bf16[1,128,2,2048]{3,1,2,0:T(8,128)(2,1)}) %all-gather.5.cloned.1.call-update) | async-done | bytes 1048592 | tf_op jit(solution)/shard_map/all_gather | solution.py:61
  179.2 2.3 fusion.127
  181.4 6.3 %collective-permute-start.2 = (bf16[1,128,2048]{2,1,0:T(8,128)(2,1)}, bf16[1,128,2048]{2,1,0:T(8,128)(2,1)}, u32[]{:S(2)}, u32[]{:S(2)}) collective-permute-start(bf16[1,128,2048]{2,1,0:T(8,128)(2,1)} %get-tuple-element.18), channel_id=1, source_target_pairs={{0,8},{8,16},{16,24},{24,32},{32,40},{40,48},{48,56},{56,64},{64,7... | collective-permute-start | bytes 1572872 | tf_op jit(solution)/shard_map/ppermute | solution.py:27
  187.7 0.5 fusion.125
  188.2 0.1 fusion.126
  188.3 0.1 pad_maximum_fusion.9
  188.4 0.2 pad_maximum_fusion.8
  188.6 9.8 %slice.269 = bf16[1,128,1,1024]{3,1,2,0:T(8,128)(2,1)} slice(bf16[1,128,1,2048]{3,1,2,0:T(8,128)(2,1)S(1)} %pad_maximum_fusion.9), slice={[0:1:1], [0:128:1], [0:1:1], [0:2048:2]} | slice | bytes 524288 | tf_op jit(solution)/shard_map/slice | solution.py:69
  198.4 9.0 %slice.263 = bf16[1,128,1,1024]{3,1,2,0:T(8,128)(2,1)S(1)} slice(bf16[1,128,1,2048]{3,1,2,0:T(8,128)(2,1)S(1)} %pad_maximum_fusion.8), slice={[0:1:1], [0:128:1], [0:1:1], [0:2048:2]} | slice | bytes 524288 | tf_op jit(solution)/shard_map/slice | solution.py:69
  207.4 0.1 pad_maximum_fusion.7
  207.5 9.0 %slice.259 = bf16[1,128,1,1024]{3,1,2,0:T(8,128)(2,1)S(1)} slice(bf16[1,128,1,2048]{3,1,2,0:T(8,128)(2,1)S(1)} %pad_maximum_fusion.7), slice={[0:1:1], [0:128:1], [0:1:1], [0:2048:2]} | slice | bytes 524288 | tf_op jit(solution)/shard_map/slice | solution.py:69
  216.4 0.2 pad_maximum_fusion.6
  216.7 9.0 %slice.252 = bf16[1,128,1,1024]{3,1,2,0:T(8,128)(2,1)S(1)} slice(bf16[1,128,1,2048]{3,1,2,0:T(8,128)(2,1)S(1)} %pad_maximum_fusion.6), slice={[0:1:1], [0:128:1], [0:1:1], [0:2048:2]} | slice | bytes 524288 | tf_op jit(solution)/shard_map/slice | solution.py:69
  225.7 9.0 %slice.255 = bf16[1,128,1,1024]{3,1,2,0:T(8,128)(2,1)S(1)} slice(bf16[1,128,1,2048]{3,1,2,0:T(8,128)(2,1)S(1)} %get-tuple-element.19), slice={[0:1:1], [0:128:1], [0:1:1], [0:2048:2]} | slice | bytes 524288 | tf_op jit(solution)/shard_map/slice | solution.py:69
  234.7 9.2 %slice.265 = bf16[1,128,1,1024]{3,1,2,0:T(8,128)(2,1)S(1)} slice(bf16[1,128,1,2048]{3,1,2,0:T(8,128)(2,1)S(1)} %get-tuple-element.17), slice={[0:1:1], [0:128:1], [0:1:1], [0:2048:2]} | slice | bytes 524288 | tf_op jit(solution)/shard_map/slice | solution.py:69
  243.9 1.1 pad_bitcast_fusion
  245.0 0.3 copy.14
  245.3 6.2 %gather_fusion.2 = bf16[2048,128]{1,0:T(8,128)(2,1)S(1)} fusion(bf16[128,2049]{0,1:T(8,128)(2,1)S(1)} %copy.14, s32[2048]{0:T(1024)S(1)} %fusion.97), kind=kCustom, calls=%fused_computation.2.clone | custom fusion | bytes 1056768 | tf_op jit(solution)/shard_map/jit(_take)/gather | solution.py:32
  251.4 0.3 fusion.42
  251.8 0.2 fusion.130
  252.0 0.8 slice.244
  252.9 0.8 slice.248
  253.7 0.1 pad_maximum_fusion.4
  253.8 0.8 slice.242
  254.7 0.2 fusion.65
  254.8 0.2 convolution_add_fusion.15
  255.0 0.2 convolution_add_fusion.14
  255.2 0.2 convolution_add_fusion.13
  255.4 0.2 convolution_add_fusion.12
  255.6 0.2 convolution_add_fusion.11
  255.8 0.2 convolution_add_fusion.10
  255.9 0.2 convolution_add_fusion.9
  256.1 0.3 copy-done.2
  256.4 0.8 fusion.76
  (24 shorter events, 0.2 us)
Async XLA Ops:
  7.2 75.3 %all-gather.3.cloned.1.call-start = ((), (), s32[]{:S(2)}) async-start(), calls=%async_computation | async-start | bytes 1179648 | tf_op jit(solution)/shard_map/all_gather | solution.py:40
  8.8 170.3 %all-gather.5.cloned.1.call-start = ((), (), s32[]{:S(2)}) async-start(), calls=%async_computation.1 | async-start | bytes 1179648 | tf_op jit(solution)/shard_map/all_gather | solution.py:61
  10.3 80.7 %copy-start.4 = (s32[1,2048]{1,0:T(1,128)S(1)}, s32[1,2048]{1,0:T(1,128)}, u32[]{:S(2)}) copy-start(s32[1,2048]{1,0:T(1,128)} %param.11) | copy-start | bytes 24580
  82.5 10.4 %copy-start = (bf16[1,128,2,2048]{3,1,2,0:T(8,128)(2,1)S(1)}, bf16[1,128,2,2048]{3,1,2,0:T(8,128)(2,1)}, u32[]{:S(2)}) copy-start(bf16[1,128,2,2048]{3,1,2,0:T(8,128)(2,1)} %all-gather.3.cloned.1.call-done) | copy-start | bytes 3145732
  84.7 12.4 %collective-permute-start = (bf16[1,128,1,2048]{3,1,2,0:T(8,128)(2,1)S(1)}, bf16[1,128,1,2048]{3,1,2,0:T(8,128)(2,1)S(1)}, u32[]{:S(2)}, u32[]{:S(2)}) collective-permute-start(bf16[1,128,1,2048]{3,1,2,0:T(8,128)(2,1)S(1)} %get-tuple-element.25), channel_id=1, source_target_pairs={{0,8},{8,16},{16,24},{24,32},{32,40},{40,48},{48,56},{56,64},{64,7... | collective-permute-start | bytes 1572872 | tf_op jit(solution)/shard_map/ppermute | solution.py:15
  91.0 12.8 %collective-permute-start.1 = (bf16[1,128,1,2048]{3,1,2,0:T(8,128)(2,1)}, bf16[1,128,1,2048]{3,1,2,0:T(8,128)(2,1)S(1)}, u32[]{:S(2)}, u32[]{:S(2)}) collective-permute-start(bf16[1,128,1,2048]{3,1,2,0:T(8,128)(2,1)} %get-tuple-element.24), channel_id=1, source_target_pairs={{8,0},{16,8},{24,16},{32,24},{40,32},{48,40},{56,48},{64,56},{72,6... | collective-permute-start | bytes 1572872 | tf_op jit(solution)/shard_map/ppermute | solution.py:17
  110.7 1.4 copy-start.5
  114.7 0.7 copy-start.6
  179.1 8.6 %copy-start.1 = (bf16[1,128,2,2048]{3,1,2,0:T(8,128)(2,1)S(1)}, bf16[1,128,2,2048]{3,1,2,0:T(8,128)(2,1)}, u32[]{:S(2)}) copy-start(bf16[1,128,2,2048]{3,1,2,0:T(8,128)(2,1)} %all-gather.5.cloned.1.call-done) | copy-start | bytes 3145732
  181.4 62.4 %collective-permute-start.2 = (bf16[1,128,2048]{2,1,0:T(8,128)(2,1)}, bf16[1,128,2048]{2,1,0:T(8,128)(2,1)}, u32[]{:S(2)}, u32[]{:S(2)}) collective-permute-start(bf16[1,128,2048]{2,1,0:T(8,128)(2,1)} %get-tuple-element.18), channel_id=1, source_target_pairs={{0,8},{8,16},{16,24},{24,32},{32,40},{40,48},{48,56},{56,64},{64,7... | collective-permute-start | bytes 1572872 | tf_op jit(solution)/shard_map/ppermute | solution.py:27
  252.9 1.8 copy-start.3
  255.4 1.0 copy-start.2
  255.4 0.9 copy-start.7
Sparse Core Ops, SparseCore 0:
  11.8 70.6 all-gather.2
  116.5 62.6 all-gather.4
where the time goes:
time: 264 us
  waiting for transfers between devices  137 us (52%)
  local copies, waits for them, and re-layouts  87.6 us (33%)
  starting transfers between devices  14.6 us (6%)
  between operations  14.4 us (5%)
  matrix products  5.98 us (2%)
  other arithmetic  4.09 us (2%)
    all_gather x1, waiting for transfers between devices, per_device(): gathered = lax.all_gather(features, 'chan', axis=1, tiled=True)  72.2 us
    all_gather x1, waiting for transfers between devices, per_device(): gathered_hidden = lax.all_gather(hidden, 'chan', axis=1, tiled=True)  61.1 us
    slice x13, local copies, waits for them, and re-layouts, per_device(): jnp.roll(stacked[:, :, row_step:row_step + row_count:2, :], 1 - col_step,...  58.1 us
    gather x5, local copies, waits for them, and re-layouts, remap_row(): jnp.take(jnp.concatenate([source_row, zero_col], axis=-1), table, axis=-1)  19 us
    ppermute x1, starting transfers between devices, shifted_2(): return lax.ppermute(array, axis, pairs)  6.29 us
    ppermute x1, starting transfers between devices, with_halo(): lax.ppermute(tail, axis, [(i, (i + 1) % count) for i in range(ends)])  6.29 us
  transfers between devices with their start and end apart: 5, of which 3 were waited for; matrix products, arithmetic and copies ran while one was open for 25% of the time, Pallas kernels for 0%

commit v1 on v0

--- a/solution.py
+++ b/solution.py
@@ -37,7 +37,9 @@
     cycle_width = features.shape[3]
     upper_map = top_map[0]
     lower_map = bottom_map[0]
-    gathered = lax.all_gather(features, "chan", axis=1, tiled=True)
+    gathered = jnp.concatenate(
+        lax.all_to_all(jnp.stack([features] * lax.axis_size("chan")), "chan", 0, 0), axis=1
+    )
     framed = with_halo(gathered, (("space", 2),), 1)
     above_row = remap_row(framed[:, :, 0, :], upper_map)
     below_row = remap_row(framed[:, :, row_count + 1, :], lower_map)

time: 264 us -> 233 us (0.88)
  waiting for transfers between devices: 137 us -> 95.4 us
  starting transfers between devices: 14.6 us -> 26.9 us
    all_gather x1 -> x0, waiting for transfers between devices: 72.2 us -> none  [per_device(): gathered = lax.all_gather(features, 'chan', axis=1, tiled=True)]
    all_to_all x0 -> x1, waiting for transfers between devices: none -> 18.9 us  [per_device(): lax.all_to_all(jnp.stack([features] * lax.axis_size('chan')), 'chan', 0, 0)]
    all_to_all x0 -> x1, starting transfers between devices: none -> 12.6 us  [per_device(): lax.all_to_all(jnp.stack([features] * lax.axis_size('chan')), 'chan', 0, 0)]
    all_gather x1, waiting for transfers between devices: 61.1 us -> 72.5 us  [per_device(): gathered_hidden = lax.all_gather(hidden, 'chan', axis=1, tiled=True)]
  transfers between devices with their start and end apart: 5 -> 5, of which waited for: 3 -> 3; matrix products, arithmetic and copies ran while one was open for 25% -> 28% of each run, Pallas kernels for 0% -> 0%
where the time goes in v1:
time: 233 us; the launch traced here: 232 us
  waiting for transfers between devices  95.4 us (41%)
  local copies, waits for them, and re-layouts  86.9 us (37%)
  starting transfers between devices  26.9 us (12%)
  between operations  14.4 us (6%)
  matrix products  6 us (3%)
  other arithmetic  2.7 us (1%)
    all_gather x1, waiting for transfers between devices, per_device(): gathered_hidden = lax.all_gather(hidden, 'chan', axis=1, tiled=True)  72.5 us
    slice x13, local copies, waits for them, and re-layouts, per_device(): jnp.roll(stacked[:, :, row_step:row_step + row_count:2, :], 1 - col_step,...  58.1 us
    gather x5, local copies, waits for them, and re-layouts, remap_row(): jnp.take(jnp.concatenate([source_row, zero_col], axis=-1), table, axis=-1)  19 us
    all_to_all x1, waiting for transfers between devices, per_device(): lax.all_to_all(jnp.stack([features] * lax.axis_size('chan')), 'chan', 0, 0)  18.9 us
    all_to_all x1, starting transfers between devices, per_device(): lax.all_to_all(jnp.stack([features] * lax.axis_size('chan')), 'chan', 0, 0)  12.6 us
    ppermute x1, starting transfers between devices, shifted_2(): return lax.ppermute(array, axis, pairs)  6.29 us
    ppermute x1, starting transfers between devices, with_halo(): lax.ppermute(tail, axis, [(i, (i + 1) % count) for i in range(ends)])  6.1 us
  transfers between devices with their start and end apart: 5, of which 3 were waited for; matrix products, arithmetic and copies ran while one was open for 28% of the time, Pallas kernels for 0%

profile of v1, /device:TPU:25, one launch (start us, length us, event | category | flops | bytes accessed | tf_op | source)
XLA Modules:
  0.0 232.4 jit_solution(6403654930126534579)
XLA Ops:
  7.2 0.9 copy.16
  8.1 1.1 stack.2
  9.2 12.6 %all-to-all-start = ((bf16[8,1,16,2,2048]{4,2,3,1,0:T(8,128)(2,1)}), bf16[8,1,16,2,2048]{4,2,3,1,0:T(8,128)(2,1)S(1)}, u32[]{:S(2)}, u32[]{:S(2)}) async-start(bf16[8,1,16,2,2048]{4,2,3,1,0:T(8,128)(2,1)} %stack.2), calls=%async_computation | async-start | bytes 2097152 | tf_op jit(solution)/shard_map/all_to_all | solution.py:41
  21.8 0.0 all-gather.2.cloned.1.call-start
  21.9 18.9 %all-to-all-done = bf16[8,1,16,2,2048]{4,2,3,1,0:T(8,128)(2,1)S(1)} async-done(((bf16[8,1,16,2,2048]{4,2,3,1,0:T(8,128)(2,1)}), bf16[8,1,16,2,2048]{4,2,3,1,0:T(8,128)(2,1)S(1)}, u32[]{:S(2)}, u32[]{:S(2)}) %all-to-all-start) | async-done | bytes 1048608 | tf_op jit(solution)/shard_map/all_to_all | solution.py:41
  40.8 0.1 copy.17
  40.9 0.9 fusion.127
  41.8 6.1 %collective-permute-start = (bf16[1,128,1,2048]{3,1,2,0:T(8,128)(2,1)S(1)}, bf16[1,128,1,2048]{3,1,2,0:T(8,128)(2,1)S(1)}, u32[]{:S(2)}, u32[]{:S(2)}) collective-permute-start(bf16[1,128,1,2048]{3,1,2,0:T(8,128)(2,1)S(1)} %get-tuple-element.27), channel_id=1, source_target_pairs={{0,8},{8,16},{16,24},{24,32},{32,40},{40,48},{48,56},{56,64},{64,7... | collective-permute-start | bytes 1572872 | tf_op jit(solution)/shard_map/ppermute | solution.py:15
  47.9 1.9 collective-permute-start.1
  49.9 0.1 fusion.128
  49.9 4.0 %collective-permute-done = bf16[1,128,1,2048]{3,1,2,0:T(8,128)(2,1)S(1)} collective-permute-done((bf16[1,128,1,2048]{3,1,2,0:T(8,128)(2,1)S(1)}, bf16[1,128,1,2048]{3,1,2,0:T(8,128)(2,1)S(1)}, u32[]{:S(2)}, u32[]{:S(2)}) %collective-permute-start) | collective-permute-done | bytes 524320 | tf_op jit(solution)/shard_map/ppermute | solution.py:15
  54.0 0.3 copy.18
  54.3 6.2 %gather_fusion = bf16[2048,128]{1,0:T(8,128)(2,1)S(1)} fusion(bf16[128,2049]{0,1:T(8,128)(2,1)S(1)} %copy.18, s32[2048]{0:T(1024)S(1)} %fusion.96), kind=kCustom, calls=%fused_computation.clone | custom fusion | bytes 1056768 | tf_op jit(solution)/shard_map/jit(_take)/gather | solution.py:32
  60.5 0.2 copy.19
  60.8 0.3 copy.21
  61.1 6.2 %gather_fusion.1 = bf16[2048,128]{1,0:T(8,128)(2,1)S(1)} fusion(bf16[128,2049]{0,1:T(8,128)(2,1)S(1)} %copy.21, s32[2048]{0:T(1024)S(1)} %fusion.97), kind=kCustom, calls=%fused_computation.1.clone | custom fusion | bytes 1056768 | tf_op jit(solution)/shard_map/jit(_take)/gather | solution.py:32
  67.3 0.2 copy.22
  67.5 0.1 fusion.42
  67.6 1.4 fusion.6
  69.1 0.5 fusion.30
  69.6 0.3 convolution_add_fusion.7
  69.8 0.3 convolution_add_fusion.6
  70.1 0.5 convolution_add_fusion.5
  70.6 0.3 convolution_add_fusion.4
  70.9 0.3 convolution_add_fusion.3
  71.1 0.5 convolution_add_fusion.2
  71.6 0.3 convolution_add_fusion.1
  71.9 0.4 copy-done.6
  72.3 1.0 fusion.53
  73.3 1.7 copy.24
  75.0 72.5 %all-gather.2.cloned.1.call-done = bf16[1,128,2,2048]{3,1,2,0:T(8,128)(2,1)} async-done(((bf16[1,16,2,2048]{3,1,2,0:T(8,128)(2,1)}), bf16[1,128,2,2048]{3,1,2,0:T(8,128)(2,1)}) %all-gather.2.cloned.1.call-update) | async-done | bytes 1048592 | tf_op jit(solution)/shard_map/all_gather | solution.py:63
  147.5 2.3 fusion.126
  149.7 6.3 %collective-permute-start.2 = (bf16[1,128,2048]{2,1,0:T(8,128)(2,1)}, bf16[1,128,2048]{2,1,0:T(8,128)(2,1)}, u32[]{:S(2)}, u32[]{:S(2)}) collective-permute-start(bf16[1,128,2048]{2,1,0:T(8,128)(2,1)} %get-tuple-element.20), channel_id=1, source_target_pairs={{0,8},{8,16},{16,24},{24,32},{32,40},{40,48},{48,56},{56,64},{64,7... | collective-permute-start | bytes 1572872 | tf_op jit(solution)/shard_map/ppermute | solution.py:27
  156.0 0.5 fusion.124
  156.5 0.1 fusion.125
  156.6 0.1 pad_maximum_fusion.9
  156.7 0.2 pad_maximum_fusion.8
  156.9 9.8 %slice.269 = bf16[1,128,1,1024]{3,1,2,0:T(8,128)(2,1)} slice(bf16[1,128,1,2048]{3,1,2,0:T(8,128)(2,1)S(1)} %pad_maximum_fusion.9), slice={[0:1:1], [0:128:1], [0:1:1], [0:2048:2]} | slice | bytes 524288 | tf_op jit(solution)/shard_map/slice | solution.py:71
  166.7 9.0 %slice.263 = bf16[1,128,1,1024]{3,1,2,0:T(8,128)(2,1)S(1)} slice(bf16[1,128,1,2048]{3,1,2,0:T(8,128)(2,1)S(1)} %pad_maximum_fusion.8), slice={[0:1:1], [0:128:1], [0:1:1], [0:2048:2]} | slice | bytes 524288 | tf_op jit(solution)/shard_map/slice | solution.py:71
  175.7 0.1 pad_maximum_fusion.7
  175.8 9.0 %slice.259 = bf16[1,128,1,1024]{3,1,2,0:T(8,128)(2,1)S(1)} slice(bf16[1,128,1,2048]{3,1,2,0:T(8,128)(2,1)S(1)} %pad_maximum_fusion.7), slice={[0:1:1], [0:128:1], [0:1:1], [0:2048:2]} | slice | bytes 524288 | tf_op jit(solution)/shard_map/slice | solution.py:71
  184.8 0.2 pad_maximum_fusion.6
  185.0 9.0 %slice.252 = bf16[1,128,1,1024]{3,1,2,0:T(8,128)(2,1)S(1)} slice(bf16[1,128,1,2048]{3,1,2,0:T(8,128)(2,1)S(1)} %pad_maximum_fusion.6), slice={[0:1:1], [0:128:1], [0:1:1], [0:2048:2]} | slice | bytes 524288 | tf_op jit(solution)/shard_map/slice | solution.py:71
  194.0 9.0 %slice.255 = bf16[1,128,1,1024]{3,1,2,0:T(8,128)(2,1)S(1)} slice(bf16[1,128,1,2048]{3,1,2,0:T(8,128)(2,1)S(1)} %get-tuple-element.21), slice={[0:1:1], [0:128:1], [0:1:1], [0:2048:2]} | slice | bytes 524288 | tf_op jit(solution)/shard_map/slice | solution.py:71
  203.0 9.2 %slice.265 = bf16[1,128,1,1024]{3,1,2,0:T(8,128)(2,1)S(1)} slice(bf16[1,128,1,2048]{3,1,2,0:T(8,128)(2,1)S(1)} %get-tuple-element.19), slice={[0:1:1], [0:128:1], [0:1:1], [0:2048:2]} | slice | bytes 524288 | tf_op jit(solution)/shard_map/slice | solution.py:71
  212.2 1.1 pad_bitcast_fusion
  213.3 0.3 copy.23
  213.6 6.2 %gather_fusion.2 = bf16[2048,128]{1,0:T(8,128)(2,1)S(1)} fusion(bf16[128,2049]{0,1:T(8,128)(2,1)S(1)} %copy.23, s32[2048]{0:T(1024)S(1)} %fusion.96), kind=kCustom, calls=%fused_computation.2.clone | custom fusion | bytes 1056768 | tf_op jit(solution)/shard_map/jit(_take)/gather | solution.py:32
  219.8 0.3 fusion.41
  220.1 0.2 fusion.129
  220.3 0.8 slice.244
  221.2 0.8 slice.248
  222.0 0.1 pad_maximum_fusion.4
  222.2 0.8 slice.242
  223.0 0.2 fusion.64
  223.2 0.2 convolution_add_fusion.15
  223.4 0.2 convolution_add_fusion.14
  223.6 0.2 convolution_add_fusion.13
  223.8 0.2 convolution_add_fusion.12
  223.9 0.2 convolution_add_fusion.11
  224.1 0.2 convolution_add_fusion.10
  224.3 0.2 convolution_add_fusion.9
  224.4 0.3 copy-done.1
  224.7 0.8 fusion.75
  (25 shorter events, 0.2 us)
Async XLA Ops:
  9.2 12.6 %copy-start.3 = (s32[1,2048]{1,0:T(1,128)S(1)}, s32[1,2048]{1,0:T(1,128)}, u32[]{:S(2)}) copy-start(s32[1,2048]{1,0:T(1,128)} %param.10) | copy-start | bytes 24580
  9.2 31.5 %all-to-all-start = ((bf16[8,1,16,2,2048]{4,2,3,1,0:T(8,128)(2,1)}), bf16[8,1,16,2,2048]{4,2,3,1,0:T(8,128)(2,1)S(1)}, u32[]{:S(2)}, u32[]{:S(2)}) async-start(bf16[8,1,16,2,2048]{4,2,3,1,0:T(8,128)(2,1)} %stack.2), calls=%async_computation | async-start | bytes 2097152 | tf_op jit(solution)/shard_map/all_to_all | solution.py:41
  21.8 125.7 %all-gather.2.cloned.1.call-start = ((), (), s32[]{:S(2)}) async-start(), calls=%async_computation.1 | async-start | bytes 1179648 | tf_op jit(solution)/shard_map/all_gather | solution.py:63
  40.9 7.0 %copy-start.4 = (s32[1,2048]{1,0:T(1,128)S(1)}, s32[1,2048]{1,0:T(1,128)}, u32[]{:S(2)}) copy-start(s32[1,2048]{1,0:T(1,128)} %param.11) | copy-start | bytes 24580
  41.8 12.2 %collective-permute-start = (bf16[1,128,1,2048]{3,1,2,0:T(8,128)(2,1)S(1)}, bf16[1,128,1,2048]{3,1,2,0:T(8,128)(2,1)S(1)}, u32[]{:S(2)}, u32[]{:S(2)}) collective-permute-start(bf16[1,128,1,2048]{3,1,2,0:T(8,128)(2,1)S(1)} %get-tuple-element.27), channel_id=1, source_target_pairs={{0,8},{8,16},{16,24},{24,32},{32,40},{40,48},{48,56},{56,64},{64,7... | collective-permute-start | bytes 1572872 | tf_op jit(solution)/shard_map/ppermute | solution.py:15
  47.9 12.8 %collective-permute-start.1 = (bf16[1,128,1,2048]{3,1,2,0:T(8,128)(2,1)}, bf16[1,128,1,2048]{3,1,2,0:T(8,128)(2,1)S(1)}, u32[]{:S(2)}, u32[]{:S(2)}) collective-permute-start(bf16[1,128,1,2048]{3,1,2,0:T(8,128)(2,1)} %get-tuple-element.26), channel_id=1, source_target_pairs={{8,0},{16,8},{24,16},{32,24},{40,32},{48,40},{56,48},{64,56},{72,6... | collective-permute-start | bytes 1572872 | tf_op jit(solution)/shard_map/ppermute | solution.py:17
  67.6 1.4 copy-start.5
  71.6 0.7 copy-start.6
  147.5 8.6 %copy-start = (bf16[1,128,2,2048]{3,1,2,0:T(8,128)(2,1)S(1)}, bf16[1,128,2,2048]{3,1,2,0:T(8,128)(2,1)}, u32[]{:S(2)}) copy-start(bf16[1,128,2,2048]{3,1,2,0:T(8,128)(2,1)} %all-gather.2.cloned.1.call-done) | copy-start | bytes 3145732
  149.7 62.5 %collective-permute-start.2 = (bf16[1,128,2048]{2,1,0:T(8,128)(2,1)}, bf16[1,128,2048]{2,1,0:T(8,128)(2,1)}, u32[]{:S(2)}, u32[]{:S(2)}) collective-permute-start(bf16[1,128,2048]{2,1,0:T(8,128)(2,1)} %get-tuple-element.20), channel_id=1, source_target_pairs={{0,8},{8,16},{16,24},{24,32},{32,40},{40,48},{48,56},{56,64},{64,7... | collective-permute-start | bytes 1572872 | tf_op jit(solution)/shard_map/ppermute | solution.py:27
  221.2 1.8 copy-start.2
  223.7 1.0 copy-start.1
  223.8 0.9 copy-start.7
Sparse Core Ops, SparseCore 0:
  73.4 74.0 all-gather.1
